TPU v7x, 512 devices: a whole 4x8x8 slice. The times are simulated.
512 devices in a mesh: dp: 4 (over z_lo, core), ctx: 128 (over x, y, z_hi).
Axes of the slice: x: 4, y: 8, z: 8 (z_hi: 4, z_lo: 2; z = z_hi * 2 + z_lo), core: 2. Of those that a mesh axis runs over, the one named last changes fastest.
Arguments:
- query: bfloat16 [4, 32768, 1024], P('dp', 'ctx'), may hold values from -150 to 150
- key: bfloat16 [4, 32768, 1024], P('dp', 'ctx'), may hold values from -3 to 3
- value: bfloat16 [4, 32768, 1024], P('dp', 'ctx'), may hold values from -6 to 6
- grad_out: bfloat16 [4, 32768, 1024], P('dp', 'ctx'), may hold values from -30 to 30
- clause: int32 [4, 32768], P('dp', 'ctx'), may hold values from 0 to 2047, never falling along the last dimension, each value on 1 to 48 neighbouring positions
- bias_table: float32 [32, 2], replicated, may hold values from -1.5 to 1.5
Outputs:
- attended: bfloat16 [4, 32768, 1024], P('dp', 'ctx')
- query_gradient: bfloat16 [4, 32768, 1024], P('dp', 'ctx')
- key_gradient: bfloat16 [4, 32768, 1024], P('dp', 'ctx')
- value_gradient: bfloat16 [4, 32768, 1024], P('dp', 'ctx')
- bias_grad: float32 [32, 2], replicated
Inputs may be any that keep to these rules, and one draw needn't show every extreme that they name: Clause ids never fall along a document; a clause holds 1 to 48 tokens, and some clause holds exactly 48.
All inputs are finite; a program needn't handle non-finite values.
Results may differ from a plain program's by a relative error of at most 0.009.
Values may be sent and summed in bfloat16 or wider, within the bound.
No kernel may reach another device: no remote copies, remote signals or barrier semaphores. Data moves between devices by JAX's collectives and lax.ppermute only.
A program may use at most 128 MiB of HBM per device.

v0:
```python
import jax
import jax.numpy as jnp
from jax import lax
from jax.sharding import PartitionSpec as P

HEADS = 8
WINDOW = 512
BUCKETS = 32
DILATION_FIRST = 1
DILATION_SECOND = 8
DILATION_THIRD = 32


def swapped(block, axis, bit):
    count = lax.axis_size(axis)
    route = []
    for low in range(count):
        high = low | 1 << bit
        if high != low and high < count:
            route += [(low, high), (high, low)]
    return lax.ppermute(block, axis, route)


def shifted(value, axis, steps):
    count = lax.axis_size(axis)
    leading, last = (max(0, -steps), min(count, count - steps))
    return lax.ppermute(value, axis, [(source, source + steps) for source in range(leading, last)])


def with_halo(shard, sides, width):
    for axis, dim in sides:
        size, length = (lax.axis_size(axis), shard.shape[dim])
        up = [(i, (i + 1) % size) for i in range(size - 1)]
        down = [(j, i) for i, j in up]
        last = lax.slice_in_dim(shard, length - width, length, axis=dim)
        leading = lax.slice_in_dim(shard, 0, width, axis=dim)
        before = lax.ppermute(last, axis, up)
        after = lax.ppermute(leading, axis, down)
        shard = jnp.concatenate([before, shard, after], axis=dim)
    return shard


def sample_rows(matrix, initial_flag, dilation_rate):
    count = matrix.shape[0] // dilation_rate
    head_dim = matrix.shape[1] // HEADS
    grid = matrix.reshape(count, dilation_rate, HEADS, head_dim)
    return jnp.concatenate(
        [grid[:, 0, initial_flag], grid[:, dilation_rate // 2, initial_flag + 1]], axis=1
    )


def spread_rows(sampled, dilation_rate):
    count = sampled.shape[0]
    grid = jnp.zeros((count, dilation_rate) + sampled.shape[1:], sampled.dtype)
    grid = grid.at[:, 0, 0].set(sampled[:, 0]).at[:, dilation_rate // 2, 1].set(sampled[:, 1])
    return grid.reshape((count * dilation_rate,) + sampled.shape[1:])


def upper_half(bit):
    index = lax.axis_index("ctx")
    return index // 2**bit % 2 == 1


def double_rows(block, bits):
    for bit in range(bits):
        other = swapped(block, "ctx", bit)
        block = jnp.where(
            upper_half(bit),
            jnp.concatenate([other, block], axis=0),
            jnp.concatenate([block, other], axis=0),
        )
    return block


def halve_sums(block, bits):
    for bit in reversed(range(bits)):
        half = block.shape[0] // 2
        lower, higher = (block[:half], block[half:])
        upper = upper_half(bit)
        outgoing = jnp.where(upper, lower, higher)
        staying = jnp.where(upper, higher, lower)
        block = staying + swapped(outgoing.astype(jnp.bfloat16), "ctx", bit).astype(outgoing.dtype)
    return block


def span_rows(block, bits):
    return double_rows(block, bits)


def span_sums(block, bits):
    return halve_sums(block, bits)


def rows_side(score_matrix, every_key_rows, every_value_rows, gradient_list, score_scale):
    top = jnp.max(score_matrix, axis=-1, keepdims=True)
    raised = jnp.exp(score_matrix - top)
    totals = jnp.sum(raised, axis=-1, keepdims=True)
    shares = raised / totals
    softmax_weights = shares.astype(jnp.bfloat16)
    attended = jnp.einsum(
        "ezb,beo->zeo", softmax_weights, every_value_rows, preferred_element_type=jnp.float32
    )
    weight_gradient = jnp.einsum(
        "wvx,yvx->vwy", gradient_list, every_value_rows, preferred_element_type=jnp.float32
    )
    delta = jnp.sum(shares * weight_gradient, axis=-1, keepdims=True)
    logit_grads = shares * (weight_gradient - delta)
    score_gradient = logit_grads.astype(jnp.bfloat16)
    query_gradient = (
        jnp.einsum(
            "ezb,beo->zeo", score_gradient, every_key_rows, preferred_element_type=jnp.float32
        )
        * score_scale
    )
    return (
        attended,
        query_gradient,
        softmax_weights,
        score_gradient,
        logit_grads,
        top,
        totals,
        delta,
    )


def keys_side(softmax_weights, score_gradient, query_matrix, gradient_list, score_scale):
    key_gradient = (
        jnp.einsum("vjb,jvw->bvw", score_gradient, query_matrix, preferred_element_type=jnp.float32)
        * score_scale
    )
    value_gradient = jnp.einsum(
        "vjb,jvw->bvw", softmax_weights, gradient_list, preferred_element_type=jnp.float32
    )
    return (key_gradient, value_gradient)


def bucket_lookup(bucket, table):
    running = jnp.zeros((table.shape[1],) + bucket.shape, jnp.float32)
    for level in range(BUCKETS):
        running = jnp.where(bucket[None] == level, table[level][:, None, None], running)
    return running


def bucket_sums(bucket, logit_grads):
    totals = [
        jnp.sum(jnp.where(bucket[None] == level, logit_grads, 0.0), axis=(1, 2))
        for level in range(BUCKETS)
    ]
    return jnp.stack(totals, axis=0)


def pass_rim(rim, offset):
    return shifted(rim.astype(jnp.bfloat16), "ctx", offset).astype(rim.dtype)


def band_part(query_rows, key_rows, value_rows, grad_rows, clause_rows, table, score_scale):
    rows, width = query_rows.shape
    head_dim = width // HEADS
    wide = 2 * head_dim
    half = WINDOW // 2
    pair_rows = jnp.concatenate([key_rows[:, :wide], value_rows[:, :wide]], axis=1)
    extended, extended_clause = (
        with_halo(pair_rows, (("ctx", 0),), half),
        with_halo(clause_rows, (("ctx", 0),), half),
    )
    reach = rows + 2 * half
    nearby_key_rows = extended[:, :wide].reshape(reach, 2, head_dim)
    values_near = extended[:, wide:].reshape(reach, 2, head_dim)
    query_matrix = query_rows[:, :wide].reshape(rows, 2, head_dim)
    gradient_list = grad_rows[:, :wide].reshape(rows, 2, head_dim)
    start = lax.axis_index("ctx") * rows
    length = rows * lax.axis_size("ctx")
    local_query = jnp.arange(rows)[:, None]
    local_key = jnp.arange(reach)[None, :] - half
    global_key = start + local_key
    allowed = (jnp.abs(local_query - local_key) < half) & (global_key >= 0) & (global_key < length)
    bucket = jnp.minimum(jnp.abs(clause_rows[:, None] - extended_clause[None, :]), BUCKETS - 1)
    score_matrix = (
        jnp.einsum(
            "wvx,yvx->vwy", query_matrix, nearby_key_rows, preferred_element_type=jnp.float32
        )
        * score_scale
    )
    score_matrix = jnp.where(allowed[None], score_matrix + bucket_lookup(bucket, table), -jnp.inf)
    attended, query_gradient, softmax_weights, score_gradient, logit_grads, top, totals, delta = (
        rows_side(score_matrix, nearby_key_rows, values_near, gradient_list, score_scale)
    )
    key_gradient, value_gradient = keys_side(
        softmax_weights, score_gradient, query_matrix, gradient_list, score_scale
    )
    sums = jnp.concatenate(
        [key_gradient.reshape(reach, wide), value_gradient.reshape(reach, wide)], axis=1
    )
    own = sums[half : half + rows]
    from_next = pass_rim(sums[:half], -1)
    from_prev = pass_rim(sums[half + rows :], 1)
    own = own.at[rows - half :].add(from_next).at[:half].add(from_prev)
    own_key = own[:, :wide].reshape(rows, 2, head_dim)
    own_value = own[:, wide:].reshape(rows, 2, head_dim)
    return (attended, query_gradient, own_key, own_value, bucket_sums(bucket, logit_grads))


def dilated(
    query_rows, key_rows, value_rows, grad_rows, initial_flag, dilation_rate, bits, score_scale
):
    head_dim = query_rows.shape[1] // HEADS
    wide = 2 * head_dim
    picked_query = sample_rows(query_rows, initial_flag, dilation_rate)
    picked_key = sample_rows(key_rows, initial_flag, dilation_rate)
    picked_value = sample_rows(value_rows, initial_flag, dilation_rate)
    picked_grad = sample_rows(grad_rows, initial_flag, dilation_rate)
    count = picked_query.shape[0]
    gathered = span_rows(jnp.concatenate([picked_key, picked_value], axis=1), bits)
    gathered_rows = gathered.shape[0]
    every_key_rows = gathered[:, :wide].reshape(gathered_rows, 2, head_dim)
    every_value_rows = gathered[:, wide:].reshape(gathered_rows, 2, head_dim)
    query_matrix = picked_query.reshape(count, 2, head_dim)
    gradient_list = picked_grad.reshape(count, 2, head_dim)
    score_matrix = (
        jnp.einsum("wvx,yvx->vwy", query_matrix, every_key_rows, preferred_element_type=jnp.float32)
        * score_scale
    )
    attended, query_gradient, softmax_weights, score_gradient, logit_grads, top, totals, delta = (
        rows_side(score_matrix, every_key_rows, every_value_rows, gradient_list, score_scale)
    )
    key_gradient, value_gradient = keys_side(
        softmax_weights, score_gradient, query_matrix, gradient_list, score_scale
    )
    partial_sums = jnp.concatenate(
        [key_gradient.reshape(gathered_rows, wide), value_gradient.reshape(gathered_rows, wide)],
        axis=1,
    )
    own = span_sums(partial_sums, bits)
    own_key = own[:, :wide].reshape(count, 2, head_dim)
    own_value = own[:, wide:].reshape(count, 2, head_dim)
    return (
        spread_rows(attended, dilation_rate),
        spread_rows(query_gradient, dilation_rate),
        spread_rows(own_key, dilation_rate),
        spread_rows(own_value, dilation_rate),
    )


def shards(query, key, value, grad_out, clause, bias_table):
    query_rows = query[0]
    key_rows = key[0]
    value_rows = value[0]
    grad_rows = grad_out[0]
    clause_rows = clause[0]
    rows, width = query_rows.shape
    head_dim = width // HEADS
    score_scale = head_dim ** (-0.5)
    bucket_bit_count = lax.axis_size("ctx").bit_length() - 1
    band = band_part(
        query_rows, key_rows, value_rows, grad_rows, clause_rows, bias_table, score_scale
    )
    pieces = [band[:4]]
    for initial_flag, dilation_rate, bits in (
        (2, DILATION_FIRST, max(bucket_bit_count - 5, 1)),
        (4, DILATION_SECOND, bucket_bit_count - 2),
        (6, DILATION_THIRD, bucket_bit_count),
    ):
        pieces.append(
            dilated(
                query_rows,
                key_rows,
                value_rows,
                grad_rows,
                initial_flag,
                dilation_rate,
                bits,
                score_scale,
            )
        )
    bias_grad = lax.psum(band[4], ("dp", "ctx"))
    joined = [
        jnp.concatenate([piece[slot] for piece in pieces], axis=1)
        .reshape(1, rows, width)
        .astype(jnp.bfloat16)
        for slot in range(4)
    ]
    return (joined[0], joined[1], joined[2], joined[3], bias_grad)


def solution(mesh):
    in_specs = (
        P("dp", "ctx", None),
        P("dp", "ctx", None),
        P("dp", "ctx", None),
        P("dp", "ctx", None),
        P("dp", "ctx"),
        P(),
    )
    out_specs = (
        P("dp", "ctx", None),
        P("dp", "ctx", None),
        P("dp", "ctx", None),
        P("dp", "ctx", None),
        P(),
    )
    return jax.shard_map(shards, mesh=mesh, in_specs=in_specs, out_specs=out_specs, check_vma=False)
```

profile of v0, /device:TPU:6, one launch (start us, length us, event | category | flops | bytes accessed | tf_op | source)
XLA Modules:
  0.0 409.0 jit_solution(8975889016358861328)
XLA Ops:
  0.6 14.2 %collective-permute-start.3 = (s32[256]{0:T(256)}, s32[256]{0:T(256)}, u32[]{:S(2)}, u32[]{:S(2)}) collective-permute-start(s32[256]{0:T(256)} %bitcast.409), channel_id=1, source_target_pairs={{1,0},{2,1},{3,2},{4,3},{5,4},{6,5},{7,6},{8,7},{9,8},{10,9},{11,1... | collective-permute-start | bytes 3080 | tf_op jit(solution)/shard_map/ppermute | solution.py:38
  19.1 9.0 %collective-permute-start.1 = (bf16[256,512]{0,1:T(8,128)(2,1)}, bf16[256,512]{0,1:T(8,128)(2,1)}, u32[]{:S(2)}, u32[]{:S(2)}) collective-permute-start(bf16[256,512]{0,1:T(8,128)(2,1)} %pad_maximum_fusion.9), channel_id=1, source_target_pairs={{1,0},{2,1},{3,2},{4,3},{5,4},{6,5},{7,6},{8,7},{9,8},{10,9},{11,1... | collective-permute-start | bytes 786440 | tf_op jit(solution)/shard_map/ppermute | solution.py:38
  46.3 4.8 %collective-permute-start.6 = (bf16[32,512]{1,0:T(8,128)(2,1)S(1)}, bf16[32,512]{1,0:T(8,128)(2,1)S(1)}, u32[]{:S(2)}, u32[]{:S(2)}) collective-permute-start(bf16[32,512]{1,0:T(8,128)(2,1)S(1)} %pad_maximum_fusion.21), channel_id=1, source_target_pairs={{0,1},{1,0},{2,3},{3,2},{4,5},{5,4},{6,7},{7,6},{8,9},{9,8},{10,11... | collective-permute-start | bytes 98312 | tf_op jit(solution)/shard_map/ppermute | solution.py:21
  53.8 4.0 collective-permute-start.12
  58.5 5.1 %collective-permute-done.12 = bf16[16,512]{1,0:T(8,128)(2,1)S(1)} collective-permute-done((bf16[16,512]{1,0:T(8,128)(2,1)S(1)}, bf16[16,512]{1,0:T(8,128)(2,1)S(1)}, u32[]{:S(2)}, u32[]{:S(2)}) %collective-permute-start.12) | collective-permute-done | bytes 16416 | tf_op jit(solution)/shard_map/ppermute | solution.py:21
  65.6 5.4 %collective-permute-start.7 = (bf16[64,512]{1,0:T(8,128)(2,1)S(1)}, bf16[64,512]{1,0:T(8,128)(2,1)S(1)}, u32[]{:S(2)}, u32[]{:S(2)}) collective-permute-start(bf16[64,512]{1,0:T(8,128)(2,1)S(1)} %maximum_select_fusion.10), channel_id=1, source_target_pairs={{0,2},{2,0},{1,3},{3,1},{4,6},{6,4},{5,7},{7,5},{8,10},{10,8},{9,1... | collective-permute-start | bytes 196616 | tf_op jit(solution)/shard_map/ppermute | solution.py:21
  71.1 6.8 %collective-permute-start.14 = (bf16[64,512]{1,0:T(8,128)(2,1)S(1)}, bf16[64,512]{1,0:T(8,128)(2,1)S(1)}, u32[]{:S(2)}, u32[]{:S(2)}) collective-permute-start(bf16[64,512]{1,0:T(8,128)(2,1)S(1)} %maximum_select_fusion.11), channel_id=1, source_target_pairs={{0,8},{8,0},{1,9},{9,1},{2,10},{10,2},{3,11},{11,3},{4,12},{12,4},... | collective-permute-start | bytes 196616 | tf_op jit(solution)/shard_map/ppermute | solution.py:21
  80.6 4.3 %collective-permute-start.15 = (bf16[128,512]{1,0:T(8,128)(2,1)S(1)}, bf16[128,512]{1,0:T(8,128)(2,1)S(1)}, u32[]{:S(2)}, u32[]{:S(2)}) collective-permute-start(bf16[128,512]{1,0:T(8,128)(2,1)S(1)} %maximum_select_fusion.9), channel_id=1, source_target_pairs={{0,16},{16,0},{1,17},{17,1},{2,18},{18,2},{3,19},{19,3},{4,20},{20... | collective-permute-start | bytes 393224 | tf_op jit(solution)/shard_map/ppermute | solution.py:21
  84.9 4.9 %fusion.56 = (pred[256,768]{0,1:T(8,128)(4,1)S(1)}, pred[256,768]{0,1:T(8,128)(4,1)S(1)}, pred[256,768]{0,1:T(8,128)(4,1)S(1)}, pred[256,768]{0,1:T(8,128)(4,1)S...) fusion(s32[768]{0:T(1024)S(1)} %pad_add_fusion, ...), kind=kLoop, calls=%fused_computation.134 | loop fusion | flops 6881280 | bytes 6295552 | tf_op jit(solution)/shard_map/eq | solution.py:141
  90.2 3.0 collective-permute-start.9
  93.6 7.5 %collective-permute-start.16 = (bf16[256,512]{1,0:T(8,128)(2,1)S(1)}, bf16[256,512]{1,0:T(8,128)(2,1)}, u32[]{:S(2)}, u32[]{:S(2)}) collective-permute-start(bf16[256,512]{1,0:T(8,128)(2,1)S(1)} %maximum_select_fusion.7), channel_id=1, source_target_pairs={{0,32},{32,0},{1,33},{33,1},{2,34},{34,2},{3,35},{35,3},{4,36},{36... | collective-permute-start | bytes 786440 | tf_op jit(solution)/shard_map/ppermute | solution.py:21
  103.5 5.7 %fusion.9 = f32[2,256,768]{1,2,0:T(8,128)S(1)} fusion(bf16[768,2,128]{0,2,1:T(8,128)(2,1)S(1)} %bitcast.347, bf16[256,2,128]{0,2,1:T(8,128)(2,1)S(1)} %bitcast.361, f32[2]{0:T(128)S(1)} %copy-done.182, f32[2]{0:T(128)S(1)} %copy-done.183, f32[2]{0:T(128)S(1)} %copy-done.121, f32[2]{0:T(128)S(1)} %copy-done.122, f32[2]{0:T(128)S(1)} %copy-done.123, ...), kind=kOutput, calls=%fused_computation.25 | convolution fusion | flops 114425856 | bytes 8585472 | tf_op jit(solution)/shard_map/wvx,yvx->vwy/dot_general | solution.py:180
  115.8 5.5 %select_reduce_fusion = (f32[2]{0:T(128)}, f32[2]{0:T(128)}, f32[2]{0:T(128)}, f32[2]{0:T(128)}, f32[2]{0:T(128)}, /*index=5*/f32[2]{0:T(128)}, f32[2]{0:T(128)}...) fusion(pred[256,768]{0,1:T(8,128)(4,1)S(1)} %copy-done.39, ...), kind=kLoop, calls=%fused_computation.26 | loop fusion | flops 15335388 | bytes 8261776 | tf_op jit(solution)/shard_map/reduce_sum | solution.py:147
  121.4 4.4 %select_reduce_fusion.18 = (f32[2]{0:T(128)}, f32[2]{0:T(128)}, f32[2]{0:T(128)}, f32[2]{0:T(128)}, f32[2]{0:T(128)}, /*index=5*/f32[2]{0:T(128)}, f32[2]{0:T(12...) fusion(f32[2,256,768]{1,2,0:T(8,128)S(1)} %get-tuple-element.442, ...), kind=kLoop, calls=%fused_computation.44 | loop fusion | flops 11010020 | bytes 4325488 | tf_op jit(solution)/shard_map/reduce_sum | solution.py:147
  128.5 3.1 fusion.15
  131.5 5.1 %collective-permute-start.18 = (bf16[256,512]{0,1:T(8,128)(2,1)}, bf16[256,512]{0,1:T(8,128)(2,1)}, u32[]{:S(2)}, u32[]{:S(2)}) collective-permute-start(bf16[256,512]{0,1:T(8,128)(2,1)} %get-tuple-element.449), channel_id=1, source_target_pairs={{1,0},{2,1},{3,2},{4,3},{5,4},{6,5},{7,6},{8,7},{9,8},{10,9},{11,1... | collective-permute-start | bytes 786440 | tf_op jit(solution)/shard_map/ppermute | solution.py:27
  139.7 4.6 %collective-permute-start.5 = (bf16[512,512]{0,1:T(8,128)(2,1)S(1)}, bf16[512,512]{0,1:T(8,128)(2,1)}, u32[]{:S(2)}, u32[]{:S(2)}) collective-permute-start(bf16[512,512]{0,1:T(8,128)(2,1)S(1)} %maximum_select_fusion.3), channel_id=1, source_target_pairs={{0,2},{2,0},{1,3},{3,1},{4,6},{6,4},{5,7},{7,5},{8,10},{10,8},{9,1... | collective-permute-start | bytes 1572872 | tf_op jit(solution)/shard_map/ppermute | solution.py:21
  147.5 111.7 %psum.7 = f32[32,2]{0,1:T(2,128)} all-reduce(f32[32,2]{0,1:T(2,128)S(1)} %stack.131), channel_id=1, replica_groups=mesh['dp'=4,'ctx'=128] {'dp','ctx'}, use_global_device_ids=true, to_apply=%region_44.45 | all-reduce | flops 64 | bytes 512 | tf_op jit(solution)/shard_map/psum | solution.py:276
  260.3 4.0 collective-permute-start.10
  266.3 4.6 %collective-permute-start.17 = (bf16[512,512]{1,0:T(8,128)(2,1)}, bf16[512,512]{1,0:T(8,128)(2,1)}, u32[]{:S(2)}, u32[]{:S(2)}) collective-permute-start(bf16[512,512]{1,0:T(8,128)(2,1)} %maximum_select_fusion.5), channel_id=1, source_target_pairs={{0,64},{64,0},{1,65},{65,1},{2,66},{66,2},{3,67},{67,3},{4,68},{68... | collective-permute-start | bytes 1572872 | tf_op jit(solution)/shard_map/ppermute | solution.py:21
  284.7 4.5 %collective-permute-start.20 = (bf16[512,512]{0,1:T(8,128)(2,1)}, bf16[512,512]{0,1:T(8,128)(2,1)}, u32[]{:S(2)}, u32[]{:S(2)}) collective-permute-start(bf16[512,512]{0,1:T(8,128)(2,1)} %select_convert_fusion.2), channel_id=1, source_target_pairs={{0,2},{2,0},{1,3},{3,1},{4,6},{6,4},{5,7},{7,5},{8,10},{10,8},{9,1... | collective-permute-start | bytes 1572872 | tf_op jit(solution)/shard_map/ppermute | solution.py:21
  302.2 4.3 %collective-permute-start.22 = (bf16[512,512]{1,0:T(8,128)(2,1)}, bf16[512,512]{1,0:T(8,128)(2,1)}, u32[]{:S(2)}, u32[]{:S(2)}) collective-permute-start(bf16[512,512]{1,0:T(8,128)(2,1)} %select_convert_fusion.1), channel_id=1, source_target_pairs={{0,16},{16,0},{1,17},{17,1},{2,18},{18,2},{3,19},{19,3},{4,20},{20... | collective-permute-start | bytes 1572872 | tf_op jit(solution)/shard_map/ppermute | solution.py:21
  329.9 4.6 %collective-permute-start.27 = (bf16[512,512]{1,0:T(8,128)(2,1)}, bf16[512,512]{1,0:T(8,128)(2,1)}, u32[]{:S(2)}, u32[]{:S(2)}) collective-permute-start(bf16[512,512]{1,0:T(8,128)(2,1)} %select_convert_fusion), channel_id=1, source_target_pairs={{0,64},{64,0},{1,65},{65,1},{2,66},{66,2},{3,67},{67,3},{4,68},{68... | collective-permute-start | bytes 1572872 | tf_op jit(solution)/shard_map/ppermute | solution.py:21
  351.2 6.0 %collective-permute-done.21 = bf16[256,512]{0,1:T(8,128)(2,1)S(1)} collective-permute-done((bf16[256,512]{0,1:T(8,128)(2,1)S(1)}, bf16[256,512]{0,1:T(8,128)(2,1)S(1)}, u32[]{:S(2)}, u32[]{:S(2)}) %collective-permute-start.21) | collective-permute-done | bytes 262176 | tf_op jit(solution)/shard_map/ppermute | solution.py:21
  361.5 6.6 %collective-permute-start.29 = (bf16[128,512]{1,0:T(8,128)(2,1)S(1)}, bf16[128,512]{1,0:T(8,128)(2,1)S(1)}, u32[]{:S(2)}, u32[]{:S(2)}) collective-permute-start(bf16[128,512]{1,0:T(8,128)(2,1)S(1)} %select_convert_fusion.6), channel_id=1, source_target_pairs={{0,16},{16,0},{1,17},{17,1},{2,18},{18,2},{3,19},{19,3},{4,20},{20... | collective-permute-start | bytes 393224 | tf_op jit(solution)/shard_map/ppermute | solution.py:21
  368.2 4.5 %collective-permute-start.25 = (bf16[64,512]{1,0:T(8,128)(2,1)S(1)}, bf16[64,512]{1,0:T(8,128)(2,1)S(1)}, u32[]{:S(2)}, u32[]{:S(2)}) collective-permute-start(bf16[64,512]{1,0:T(8,128)(2,1)S(1)} %select_convert_fusion.9), channel_id=1, source_target_pairs={{0,2},{2,0},{1,3},{3,1},{4,6},{6,4},{5,7},{7,5},{8,10},{10,8},{9,1... | collective-permute-start | bytes 196616 | tf_op jit(solution)/shard_map/ppermute | solution.py:21
  372.9 6.8 %collective-permute-start.30 = (bf16[64,512]{1,0:T(8,128)(2,1)S(1)}, bf16[64,512]{1,0:T(8,128)(2,1)S(1)}, u32[]{:S(2)}, u32[]{:S(2)}) collective-permute-start(bf16[64,512]{1,0:T(8,128)(2,1)S(1)} %select_convert_fusion.8), channel_id=1, source_target_pairs={{0,8},{8,0},{1,9},{9,1},{2,10},{10,2},{3,11},{11,3},{4,12},{12,4},... | collective-permute-start | bytes 196616 | tf_op jit(solution)/shard_map/ppermute | solution.py:21
  379.7 4.5 %collective-permute-start.26 = (bf16[32,512]{1,0:T(8,128)(2,1)S(1)}, bf16[32,512]{1,0:T(8,128)(2,1)S(1)}, u32[]{:S(2)}, u32[]{:S(2)}) collective-permute-start(bf16[32,512]{1,0:T(8,128)(2,1)S(1)} %select_convert_fusion.11), channel_id=1, source_target_pairs={{0,1},{1,0},{2,3},{3,2},{4,5},{5,4},{6,7},{7,6},{8,9},{9,8},{10,11... | collective-permute-start | bytes 98312 | tf_op jit(solution)/shard_map/ppermute | solution.py:21
  384.4 3.0 collective-permute-start.31
  390.2 5.2 %collective-permute-start.32 = (bf16[16,512]{1,0:T(8,128)(2,1)S(1)}, bf16[16,512]{1,0:T(8,128)(2,1)S(1)}, u32[]{:S(2)}, u32[]{:S(2)}) collective-permute-start(bf16[16,512]{1,0:T(8,128)(2,1)S(1)} %select_convert_fusion.12), channel_id=1, source_target_pairs={{0,2},{2,0},{1,3},{3,1},{4,6},{6,4},{5,7},{7,5},{8,10},{10,8},{9,1... | collective-permute-start | bytes 49160 | tf_op jit(solution)/shard_map/ppermute | solution.py:21
  395.5 4.3 %collective-permute-done.32 = bf16[16,512]{1,0:T(8,128)(2,1)S(1)} collective-permute-done((bf16[16,512]{1,0:T(8,128)(2,1)S(1)}, bf16[16,512]{1,0:T(8,128)(2,1)S(1)}, u32[]{:S(2)}, u32[]{:S(2)}) %collective-permute-start.32) | collective-permute-done | bytes 16416 | tf_op jit(solution)/shard_map/ppermute | solution.py:21
  403.2 3.0 collective-permute-done.33
  (644 shorter events, 129.6 us)
Async XLA Ops:
  0.6 51.3 %collective-permute-start.3 = (s32[256]{0:T(256)}, s32[256]{0:T(256)}, u32[]{:S(2)}, u32[]{:S(2)}) collective-permute-start(s32[256]{0:T(256)} %bitcast.409), channel_id=1, source_target_pairs={{1,0},{2,1},{3,2},{4,3},{5,4},{6,5},{7,6},{8,7},{9,8},{10,9},{11,1... | collective-permute-start | bytes 3080 | tf_op jit(solution)/shard_map/ppermute | solution.py:38
  14.9 38.9 %collective-permute-start.2 = (s32[256]{0:T(256)}, s32[256]{0:T(256)}, u32[]{:S(2)}, u32[]{:S(2)}) collective-permute-start(s32[256]{0:T(256)} %bitcast.410), channel_id=1, source_target_pairs={{0,1},{1,2},{2,3},{3,4},{4,5},{5,6},{6,7},{7,8},{8,9},{9,10},{10,1... | collective-permute-start | bytes 3080 | tf_op jit(solution)/shard_map/ppermute | solution.py:37
  19.1 82.0 %collective-permute-start.1 = (bf16[256,512]{0,1:T(8,128)(2,1)}, bf16[256,512]{0,1:T(8,128)(2,1)}, u32[]{:S(2)}, u32[]{:S(2)}) collective-permute-start(bf16[256,512]{0,1:T(8,128)(2,1)} %pad_maximum_fusion.9), channel_id=1, source_target_pairs={{1,0},{2,1},{3,2},{4,3},{5,4},{6,5},{7,6},{8,7},{9,8},{10,9},{11,1... | collective-permute-start | bytes 786440 | tf_op jit(solution)/shard_map/ppermute | solution.py:38
  28.1 73.0 %collective-permute-start = (bf16[256,512]{0,1:T(8,128)(2,1)}, bf16[256,512]{0,1:T(8,128)(2,1)}, u32[]{:S(2)}, u32[]{:S(2)}) collective-permute-start(bf16[256,512]{0,1:T(8,128)(2,1)} %pad_maximum_fusion.9), channel_id=1, source_target_pairs={{0,1},{1,2},{2,3},{3,4},{4,5},{5,6},{6,7},{7,8},{8,9},{9,10},{10,1... | collective-permute-start | bytes 786440 | tf_op jit(solution)/shard_map/ppermute | solution.py:37
  31.8 14.5 %collective-permute-start.11 = (bf16[8,512]{1,0:T(8,128)(2,1)}, bf16[8,512]{1,0:T(8,128)(2,1)}, u32[]{:S(2)}, u32[]{:S(2)}) collective-permute-start(bf16[8,512]{1,0:T(8,128)(2,1)} %pad_maximum_fusion.28), channel_id=1, source_target_pairs={{0,1},{1,0},{2,3},{3,2},{4,5},{5,4},{6,7},{7,6},{8,9},{9,8},{10,11... | collective-permute-start | bytes 24584 | tf_op jit(solution)/shard_map/ppermute | solution.py:21
  46.3 19.3 %collective-permute-start.6 = (bf16[32,512]{1,0:T(8,128)(2,1)S(1)}, bf16[32,512]{1,0:T(8,128)(2,1)S(1)}, u32[]{:S(2)}, u32[]{:S(2)}) collective-permute-start(bf16[32,512]{1,0:T(8,128)(2,1)S(1)} %pad_maximum_fusion.21), channel_id=1, source_target_pairs={{0,1},{1,0},{2,3},{3,2},{4,5},{5,4},{6,7},{7,6},{8,9},{9,8},{10,11... | collective-permute-start | bytes 98312 | tf_op jit(solution)/shard_map/ppermute | solution.py:21
  51.9 86.6 %collective-permute-start.4 = (bf16[256,512]{0,1:T(8,128)(2,1)}, bf16[256,512]{0,1:T(8,128)(2,1)}, u32[]{:S(2)}, u32[]{:S(2)}) collective-permute-start(bf16[256,512]{0,1:T(8,128)(2,1)} %pad_maximum_fusion.10), channel_id=1, source_target_pairs={{0,1},{1,0},{2,3},{3,2},{4,5},{5,4},{6,7},{7,6},{8,9},{9,8},{10,11... | collective-permute-start | bytes 786440 | tf_op jit(solution)/shard_map/ppermute | solution.py:21
  53.8 9.8 %collective-permute-start.12 = (bf16[16,512]{1,0:T(8,128)(2,1)S(1)}, bf16[16,512]{1,0:T(8,128)(2,1)S(1)}, u32[]{:S(2)}, u32[]{:S(2)}) collective-permute-start(bf16[16,512]{1,0:T(8,128)(2,1)S(1)} %maximum_select_fusion.13), channel_id=1, source_target_pairs={{0,2},{2,0},{1,3},{3,1},{4,6},{6,4},{5,7},{7,5},{8,10},{10,8},{9,1... | collective-permute-start | bytes 49160 | tf_op jit(solution)/shard_map/ppermute | solution.py:21
  63.7 7.4 %collective-permute-start.13 = (bf16[32,512]{1,0:T(8,128)(2,1)S(1)}, bf16[32,512]{1,0:T(8,128)(2,1)S(1)}, u32[]{:S(2)}, u32[]{:S(2)}) collective-permute-start(bf16[32,512]{1,0:T(8,128)(2,1)S(1)} %maximum_select_fusion.12), channel_id=1, source_target_pairs={{0,4},{4,0},{1,5},{5,1},{2,6},{6,2},{3,7},{7,3},{8,12},{12,8},{9,1... | collective-permute-start | bytes 98312 | tf_op jit(solution)/shard_map/ppermute | solution.py:21
  65.6 12.3 %collective-permute-start.7 = (bf16[64,512]{1,0:T(8,128)(2,1)S(1)}, bf16[64,512]{1,0:T(8,128)(2,1)S(1)}, u32[]{:S(2)}, u32[]{:S(2)}) collective-permute-start(bf16[64,512]{1,0:T(8,128)(2,1)S(1)} %maximum_select_fusion.10), channel_id=1, source_target_pairs={{0,2},{2,0},{1,3},{3,1},{4,6},{6,4},{5,7},{7,5},{8,10},{10,8},{9,1... | collective-permute-start | bytes 196616 | tf_op jit(solution)/shard_map/ppermute | solution.py:21
  71.1 9.5 %collective-permute-start.14 = (bf16[64,512]{1,0:T(8,128)(2,1)S(1)}, bf16[64,512]{1,0:T(8,128)(2,1)S(1)}, u32[]{:S(2)}, u32[]{:S(2)}) collective-permute-start(bf16[64,512]{1,0:T(8,128)(2,1)S(1)} %maximum_select_fusion.11), channel_id=1, source_target_pairs={{0,8},{8,0},{1,9},{9,1},{2,10},{10,2},{3,11},{11,3},{4,12},{12,4},... | collective-permute-start | bytes 196616 | tf_op jit(solution)/shard_map/ppermute | solution.py:21
  77.9 12.2 %collective-permute-start.8 = (bf16[128,512]{1,0:T(8,128)(2,1)S(1)}, bf16[128,512]{1,0:T(8,128)(2,1)S(1)}, u32[]{:S(2)}, u32[]{:S(2)}) collective-permute-start(bf16[128,512]{1,0:T(8,128)(2,1)S(1)} %maximum_select_fusion.8), channel_id=1, source_target_pairs={{0,4},{4,0},{1,5},{5,1},{2,6},{6,2},{3,7},{7,3},{8,12},{12,8},{9,1... | collective-permute-start | bytes 393224 | tf_op jit(solution)/shard_map/ppermute | solution.py:21
  80.6 12.6 %collective-permute-start.15 = (bf16[128,512]{1,0:T(8,128)(2,1)S(1)}, bf16[128,512]{1,0:T(8,128)(2,1)S(1)}, u32[]{:S(2)}, u32[]{:S(2)}) collective-permute-start(bf16[128,512]{1,0:T(8,128)(2,1)S(1)} %maximum_select_fusion.9), channel_id=1, source_target_pairs={{0,16},{16,0},{1,17},{17,1},{2,18},{18,2},{3,19},{19,3},{4,20},{20... | collective-permute-start | bytes 393224 | tf_op jit(solution)/shard_map/ppermute | solution.py:21
  90.2 169.0 %collective-permute-start.9 = (bf16[256,512]{1,0:T(8,128)(2,1)S(1)}, bf16[256,512]{1,0:T(8,128)(2,1)}, u32[]{:S(2)}, u32[]{:S(2)}) collective-permute-start(bf16[256,512]{1,0:T(8,128)(2,1)S(1)} %maximum_select_fusion.6), channel_id=1, source_target_pairs={{0,8},{8,0},{1,9},{9,1},{2,10},{10,2},{3,11},{11,3},{4,12},{12,4},... | collective-permute-start | bytes 786440 | tf_op jit(solution)/shard_map/ppermute | solution.py:21
  93.6 170.7 %collective-permute-start.16 = (bf16[256,512]{1,0:T(8,128)(2,1)S(1)}, bf16[256,512]{1,0:T(8,128)(2,1)}, u32[]{:S(2)}, u32[]{:S(2)}) collective-permute-start(bf16[256,512]{1,0:T(8,128)(2,1)S(1)} %maximum_select_fusion.7), channel_id=1, source_target_pairs={{0,32},{32,0},{1,33},{33,1},{2,34},{34,2},{3,35},{35,3},{4,36},{36... | collective-permute-start | bytes 786440 | tf_op jit(solution)/shard_map/ppermute | solution.py:21
  131.5 139.3 %collective-permute-start.18 = (bf16[256,512]{0,1:T(8,128)(2,1)}, bf16[256,512]{0,1:T(8,128)(2,1)}, u32[]{:S(2)}, u32[]{:S(2)}) collective-permute-start(bf16[256,512]{0,1:T(8,128)(2,1)} %get-tuple-element.449), channel_id=1, source_target_pairs={{1,0},{2,1},{3,2},{4,3},{5,4},{6,5},{7,6},{8,7},{9,8},{10,9},{11,1... | collective-permute-start | bytes 786440 | tf_op jit(solution)/shard_map/ppermute | solution.py:27
  136.6 134.3 %collective-permute-start.19 = (bf16[256,512]{0,1:T(8,128)(2,1)}, bf16[256,512]{0,1:T(8,128)(2,1)}, u32[]{:S(2)}, u32[]{:S(2)}) collective-permute-start(bf16[256,512]{0,1:T(8,128)(2,1)} %get-tuple-element.450), channel_id=1, source_target_pairs={{0,1},{1,2},{2,3},{3,4},{4,5},{5,6},{6,7},{7,8},{8,9},{9,10},{10,1... | collective-permute-start | bytes 786440 | tf_op jit(solution)/shard_map/ppermute | solution.py:27
  139.7 133.0 %collective-permute-start.5 = (bf16[512,512]{0,1:T(8,128)(2,1)S(1)}, bf16[512,512]{0,1:T(8,128)(2,1)}, u32[]{:S(2)}, u32[]{:S(2)}) collective-permute-start(bf16[512,512]{0,1:T(8,128)(2,1)S(1)} %maximum_select_fusion.3), channel_id=1, source_target_pairs={{0,2},{2,0},{1,3},{3,1},{4,6},{6,4},{5,7},{7,5},{8,10},{10,8},{9,1... | collective-permute-start | bytes 1572872 | tf_op jit(solution)/shard_map/ppermute | solution.py:21
  260.3 30.9 %collective-permute-start.10 = (bf16[512,512]{1,0:T(8,128)(2,1)S(1)}, bf16[512,512]{1,0:T(8,128)(2,1)}, u32[]{:S(2)}, u32[]{:S(2)}) collective-permute-start(bf16[512,512]{1,0:T(8,128)(2,1)S(1)} %maximum_select_fusion.4), channel_id=1, source_target_pairs={{0,16},{16,0},{1,17},{17,1},{2,18},{18,2},{3,19},{19,3},{4,20},{20... | collective-permute-start | bytes 1572872 | tf_op jit(solution)/shard_map/ppermute | solution.py:21
  266.3 40.2 %collective-permute-start.17 = (bf16[512,512]{1,0:T(8,128)(2,1)}, bf16[512,512]{1,0:T(8,128)(2,1)}, u32[]{:S(2)}, u32[]{:S(2)}) collective-permute-start(bf16[512,512]{1,0:T(8,128)(2,1)} %maximum_select_fusion.5), channel_id=1, source_target_pairs={{0,64},{64,0},{1,65},{65,1},{2,66},{66,2},{3,67},{67,3},{4,68},{68... | collective-permute-start | bytes 1572872 | tf_op jit(solution)/shard_map/ppermute | solution.py:21
  284.7 55.7 %collective-permute-start.20 = (bf16[512,512]{0,1:T(8,128)(2,1)}, bf16[512,512]{0,1:T(8,128)(2,1)}, u32[]{:S(2)}, u32[]{:S(2)}) collective-permute-start(bf16[512,512]{0,1:T(8,128)(2,1)} %select_convert_fusion.2), channel_id=1, source_target_pairs={{0,2},{2,0},{1,3},{3,1},{4,6},{6,4},{5,7},{7,5},{8,10},{10,8},{9,1... | collective-permute-start | bytes 1572872 | tf_op jit(solution)/shard_map/ppermute | solution.py:21
  302.2 42.2 %collective-permute-start.22 = (bf16[512,512]{1,0:T(8,128)(2,1)}, bf16[512,512]{1,0:T(8,128)(2,1)}, u32[]{:S(2)}, u32[]{:S(2)}) collective-permute-start(bf16[512,512]{1,0:T(8,128)(2,1)} %select_convert_fusion.1), channel_id=1, source_target_pairs={{0,16},{16,0},{1,17},{17,1},{2,18},{18,2},{3,19},{19,3},{4,20},{20... | collective-permute-start | bytes 1572872 | tf_op jit(solution)/shard_map/ppermute | solution.py:21
  329.9 18.0 %collective-permute-start.27 = (bf16[512,512]{1,0:T(8,128)(2,1)}, bf16[512,512]{1,0:T(8,128)(2,1)}, u32[]{:S(2)}, u32[]{:S(2)}) collective-permute-start(bf16[512,512]{1,0:T(8,128)(2,1)} %select_convert_fusion), channel_id=1, source_target_pairs={{0,64},{64,0},{1,65},{65,1},{2,66},{66,2},{3,67},{67,3},{4,68},{68... | collective-permute-start | bytes 1572872 | tf_op jit(solution)/shard_map/ppermute | solution.py:21
  342.1 15.1 %collective-permute-start.21 = (bf16[256,512]{0,1:T(8,128)(2,1)S(1)}, bf16[256,512]{0,1:T(8,128)(2,1)S(1)}, u32[]{:S(2)}, u32[]{:S(2)}) collective-permute-start(bf16[256,512]{0,1:T(8,128)(2,1)S(1)} %select_convert_fusion.5), channel_id=1, source_target_pairs={{0,1},{1,0},{2,3},{3,2},{4,5},{5,4},{6,7},{7,6},{8,9},{9,8},{10,11... | collective-permute-start | bytes 786440 | tf_op jit(solution)/shard_map/ppermute | solution.py:21
  345.7 13.5 %collective-permute-start.23 = (bf16[256,512]{1,0:T(8,128)(2,1)S(1)}, bf16[256,512]{1,0:T(8,128)(2,1)S(1)}, u32[]{:S(2)}, u32[]{:S(2)}) collective-permute-start(bf16[256,512]{1,0:T(8,128)(2,1)S(1)} %select_convert_fusion.4), channel_id=1, source_target_pairs={{0,8},{8,0},{1,9},{9,1},{2,10},{10,2},{3,11},{11,3},{4,12},{12,4},... | collective-permute-start | bytes 786440 | tf_op jit(solution)/shard_map/ppermute | solution.py:21
  349.3 12.0 %collective-permute-start.28 = (bf16[256,512]{1,0:T(8,128)(2,1)S(1)}, bf16[256,512]{1,0:T(8,128)(2,1)S(1)}, u32[]{:S(2)}, u32[]{:S(2)}) collective-permute-start(bf16[256,512]{1,0:T(8,128)(2,1)S(1)} %select_convert_fusion.3), channel_id=1, source_target_pairs={{0,32},{32,0},{1,33},{33,1},{2,34},{34,2},{3,35},{35,3},{4,36},{36... | collective-permute-start | bytes 786440 | tf_op jit(solution)/shard_map/ppermute | solution.py:21
  359.4 8.7 %collective-permute-start.24 = (bf16[128,512]{1,0:T(8,128)(2,1)S(1)}, bf16[128,512]{1,0:T(8,128)(2,1)S(1)}, u32[]{:S(2)}, u32[]{:S(2)}) collective-permute-start(bf16[128,512]{1,0:T(8,128)(2,1)S(1)} %select_convert_fusion.7), channel_id=1, source_target_pairs={{0,4},{4,0},{1,5},{5,1},{2,6},{6,2},{3,7},{7,3},{8,12},{12,8},{9,1... | collective-permute-start | bytes 393224 | tf_op jit(solution)/shard_map/ppermute | solution.py:21
  361.5 11.3 %collective-permute-start.29 = (bf16[128,512]{1,0:T(8,128)(2,1)S(1)}, bf16[128,512]{1,0:T(8,128)(2,1)S(1)}, u32[]{:S(2)}, u32[]{:S(2)}) collective-permute-start(bf16[128,512]{1,0:T(8,128)(2,1)S(1)} %select_convert_fusion.6), channel_id=1, source_target_pairs={{0,16},{16,0},{1,17},{17,1},{2,18},{18,2},{3,19},{19,3},{4,20},{20... | collective-permute-start | bytes 393224 | tf_op jit(solution)/shard_map/ppermute | solution.py:21
  368.2 11.5 %collective-permute-start.25 = (bf16[64,512]{1,0:T(8,128)(2,1)S(1)}, bf16[64,512]{1,0:T(8,128)(2,1)S(1)}, u32[]{:S(2)}, u32[]{:S(2)}) collective-permute-start(bf16[64,512]{1,0:T(8,128)(2,1)S(1)} %select_convert_fusion.9), channel_id=1, source_target_pairs={{0,2},{2,0},{1,3},{3,1},{4,6},{6,4},{5,7},{7,5},{8,10},{10,8},{9,1... | collective-permute-start | bytes 196616 | tf_op jit(solution)/shard_map/ppermute | solution.py:21
  372.9 11.4 %collective-permute-start.30 = (bf16[64,512]{1,0:T(8,128)(2,1)S(1)}, bf16[64,512]{1,0:T(8,128)(2,1)S(1)}, u32[]{:S(2)}, u32[]{:S(2)}) collective-permute-start(bf16[64,512]{1,0:T(8,128)(2,1)S(1)} %select_convert_fusion.8), channel_id=1, source_target_pairs={{0,8},{8,0},{1,9},{9,1},{2,10},{10,2},{3,11},{11,3},{4,12},{12,4},... | collective-permute-start | bytes 196616 | tf_op jit(solution)/shard_map/ppermute | solution.py:21
  379.7 7.7 %collective-permute-start.26 = (bf16[32,512]{1,0:T(8,128)(2,1)S(1)}, bf16[32,512]{1,0:T(8,128)(2,1)S(1)}, u32[]{:S(2)}, u32[]{:S(2)}) collective-permute-start(bf16[32,512]{1,0:T(8,128)(2,1)S(1)} %select_convert_fusion.11), channel_id=1, source_target_pairs={{0,1},{1,0},{2,3},{3,2},{4,5},{5,4},{6,7},{7,6},{8,9},{9,8},{10,11... | collective-permute-start | bytes 98312 | tf_op jit(solution)/shard_map/ppermute | solution.py:21
  390.2 9.5 %collective-permute-start.32 = (bf16[16,512]{1,0:T(8,128)(2,1)S(1)}, bf16[16,512]{1,0:T(8,128)(2,1)S(1)}, u32[]{:S(2)}, u32[]{:S(2)}) collective-permute-start(bf16[16,512]{1,0:T(8,128)(2,1)S(1)} %select_convert_fusion.12), channel_id=1, source_target_pairs={{0,2},{2,0},{1,3},{3,1},{4,6},{6,4},{5,7},{7,5},{8,10},{10,8},{9,1... | collective-permute-start | bytes 49160 | tf_op jit(solution)/shard_map/ppermute | solution.py:21
  (186 other events, 1898.1 us)
where the time goes:
time: 416 us; the launch traced here: 409 us
  starting transfers between devices  146 us (35%)
  blocking collectives  112 us (27%)
  other arithmetic  46.6 us (11%)
  local copies, waits for them, and re-layouts  43.8 us (11%)
  matrix products  33 us (8%)
  waiting for transfers between devices  23.4 us (6%)
  between operations  4.5 us (1%)
    ppermute x28, starting transfers between devices, swapped(): return lax.ppermute(block, axis, route)  112 us
    psum x1, blocking collectives, shards(): bias_grad = lax.psum(band[4], ('dp', 'ctx'))  112 us
    ppermute x28, waiting for transfers between devices, swapped(): return lax.ppermute(block, axis, route)  23.4 us
    ppermute x2, starting transfers between devices, with_halo(): after = lax.ppermute(leading, axis, down)  23.3 us
    unnamed x386, local copies, waits for them, and re-layouts  13.6 us
    select_n x14, other arithmetic, double_rows(): jnp.where(upper_half(bit), jnp.concatenate([other, block], axis=0), jnp.c...  10.2 us
    reduce_sum x2, other arithmetic, bucket_sums(): jnp.sum(jnp.where(bucket[None] == level, logit_grads, 0.0), axis=(1, 2))  9.92 us
  transfers between devices with their start and end apart: 34, of which 9 were waited for; matrix products, arithmetic and copies ran while one was open for 29% of the time, Pallas kernels for 0%

commit v1 on v0

--- a/solution.py
+++ b/solution.py
@@ -273,7 +273,7 @@
                 score_scale,
             )
         )
-    bias_grad = lax.psum(band[4], ("dp", "ctx"))
+    bias_grad = jnp.sum(lax.all_gather(band[4], ("dp", "ctx")), axis=0)
     joined = [
         jnp.concatenate([piece[slot] for piece in pieces], axis=1)
         .reshape(1, rows, width)

time: 416 us -> 1770 us (4.25)
  the two profiles are of different devices: /device:TPU:6 before, /device:TPU:64 now
where the time goes in v1:
time: 1770 us; the launch traced here: 1760 us
  blocking collectives  1480 us (84%)
  starting transfers between devices  147 us (8%)
  other arithmetic  47.6 us (3%)
  local copies, waits for them, and re-layouts  42.1 us (2%)
  matrix products  28.9 us (2%)
    all_gather x1, blocking collectives, shards(): bias_grad = jnp.sum(lax.all_gather(band[4], ('dp', 'ctx')), axis=0)  1480 us
    ppermute x28, starting transfers between devices, swapped(): return lax.ppermute(block, axis, route)  122 us
  transfers between devices with their start and end apart: 34, of which 10 were waited for; matrix products, arithmetic and copies ran while one was open for 6% of the time, Pallas kernels for 0%

profile of v1, /device:TPU:64, one launch (start us, length us, event | category | flops | bytes accessed | tf_op | source)
XLA Modules:
  0.0 1762.0 jit_solution(7219576265690447452)
XLA Ops:
  2.1 7.3 collective-permute-start.2
  12.9 7.2 collective-permute-start
  21.9 5.3 collective-permute-start.11
  42.6 4.8 collective-permute-start.4
  47.4 9.6 collective-permute-start.12
  58.8 3.6 collective-permute-start.13
  62.4 9.4 collective-permute-start.7
  71.8 5.3 collective-permute-start.14
  79.6 7.1 collective-permute-start.15
  86.7 5.0 fusion.56
  91.8 4.4 collective-permute-start.9
  97.3 3.9 collective-permute-start.16
  102.6 5.8 fusion.9
  109.8 5.5 select_reduce_fusion
  115.4 4.4 select_reduce_fusion.18
  125.0 5.6 collective-permute-start.5
  136.2 6.2 collective-permute-start.19
  142.5 1479.0 %all-gather.1 = f32[512,32,2]{1,2,0:T(2,128)S(1)} all-gather(f32[1,32,2]{1,2,0:T(2,128)S(1)} %bitcast.414), channel_id=2, replica_groups=mesh['dp'=4,'ctx'=128] {'dp','ctx'}, dimensions={0}, use_global_device_ids=true | all-gather | bytes 131328 | tf_op jit(solution)/shard_map/all_gather | solution.py:276
  1637.5 2.5 multiply_reduce_fusion
  1656.5 8.0 collective-permute-start.22
  1679.1 2.6 copy.675
  1683.0 2.6 copy.674
  1685.6 2.5 select_convert_fusion
  1688.1 5.4 collective-permute-start.27
  1701.1 2.7 collective-permute-start.21
  1718.8 2.6 collective-permute-done.24
  1721.4 7.8 collective-permute-start.25
  1729.3 3.6 collective-permute-start.30
  1733.1 4.2 collective-permute-start.26
  1739.8 3.3 collective-permute-done.31
  1743.1 7.8 collective-permute-start.32
  1752.7 4.0 collective-permute-start.33
  (515 shorter events, 119.4 us)
Async XLA Ops:
  0.6 41.9 %collective-permute-start.3 = (s32[256]{0:T(256)}, s32[256]{0:T(256)}, u32[]{:S(2)}, u32[]{:S(2)}) collective-permute-start(s32[256]{0:T(256)} %bitcast.410), channel_id=1, source_target_pairs={{1,0},{2,1},{3,2},{4,3},{5,4},{6,5},{7,6},{8,7},{9,8},{10,9},{11,1... | collective-permute-start | bytes 3080 | tf_op jit(solution)/shard_map/ppermute | solution.py:38
  2.1 45.3 %collective-permute-start.2 = (s32[256]{0:T(256)}, s32[256]{0:T(256)}, u32[]{:S(2)}, u32[]{:S(2)}) collective-permute-start(s32[256]{0:T(256)} %bitcast.411), channel_id=1, source_target_pairs={{0,1},{1,2},{2,3},{3,4},{4,5},{5,6},{6,7},{7,8},{8,9},{9,10},{10,1... | collective-permute-start | bytes 3080 | tf_op jit(solution)/shard_map/ppermute | solution.py:37
  11.6 89.5 %collective-permute-start.1 = (bf16[256,512]{0,1:T(8,128)(2,1)}, bf16[256,512]{0,1:T(8,128)(2,1)}, u32[]{:S(2)}, u32[]{:S(2)}) collective-permute-start(bf16[256,512]{0,1:T(8,128)(2,1)} %pad_maximum_fusion.9), channel_id=1, source_target_pairs={{1,0},{2,1},{3,2},{4,3},{5,4},{6,5},{7,6},{8,7},{9,8},{10,9},{11,1... | collective-permute-start | bytes 786440 | tf_op jit(solution)/shard_map/ppermute | solution.py:38
  12.9 88.2 %collective-permute-start = (bf16[256,512]{0,1:T(8,128)(2,1)}, bf16[256,512]{0,1:T(8,128)(2,1)}, u32[]{:S(2)}, u32[]{:S(2)}) collective-permute-start(bf16[256,512]{0,1:T(8,128)(2,1)} %pad_maximum_fusion.9), channel_id=1, source_target_pairs={{0,1},{1,2},{2,3},{3,4},{4,5},{5,6},{6,7},{7,8},{8,9},{9,10},{10,1... | collective-permute-start | bytes 786440 | tf_op jit(solution)/shard_map/ppermute | solution.py:37
  21.9 17.9 %collective-permute-start.11 = (bf16[8,512]{1,0:T(8,128)(2,1)}, bf16[8,512]{1,0:T(8,128)(2,1)}, u32[]{:S(2)}, u32[]{:S(2)}) collective-permute-start(bf16[8,512]{1,0:T(8,128)(2,1)} %pad_maximum_fusion.28), channel_id=1, source_target_pairs={{0,1},{1,0},{2,3},{3,2},{4,5},{5,4},{6,7},{7,6},{8,9},{9,8},{10,11... | collective-permute-start | bytes 24584 | tf_op jit(solution)/shard_map/ppermute | solution.py:21
  39.8 22.6 %collective-permute-start.6 = (bf16[32,512]{1,0:T(8,128)(2,1)S(1)}, bf16[32,512]{1,0:T(8,128)(2,1)S(1)}, u32[]{:S(2)}, u32[]{:S(2)}) collective-permute-start(bf16[32,512]{1,0:T(8,128)(2,1)S(1)} %pad_maximum_fusion.21), channel_id=1, source_target_pairs={{0,1},{1,0},{2,3},{3,2},{4,5},{5,4},{6,7},{7,6},{8,9},{9,8},{10,11... | collective-permute-start | bytes 98312 | tf_op jit(solution)/shard_map/ppermute | solution.py:21
  42.6 81.2 %collective-permute-start.4 = (bf16[256,512]{0,1:T(8,128)(2,1)}, bf16[256,512]{0,1:T(8,128)(2,1)}, u32[]{:S(2)}, u32[]{:S(2)}) collective-permute-start(bf16[256,512]{0,1:T(8,128)(2,1)} %pad_maximum_fusion.10), channel_id=1, source_target_pairs={{0,1},{1,0},{2,3},{3,2},{4,5},{5,4},{6,7},{7,6},{8,9},{9,8},{10,11... | collective-permute-start | bytes 786440 | tf_op jit(solution)/shard_map/ppermute | solution.py:21
  47.4 11.4 collective-permute-start.12
  58.8 13.0 collective-permute-start.13
  62.4 14.8 collective-permute-start.7
  71.8 7.7 collective-permute-start.14
  77.2 14.5 collective-permute-start.8
  79.6 16.6 collective-permute-start.15
  91.8 1530.8 %collective-permute-start.9 = (bf16[256,512]{1,0:T(8,128)(2,1)S(1)}, bf16[256,512]{1,0:T(8,128)(2,1)}, u32[]{:S(2)}, u32[]{:S(2)}) collective-permute-start(bf16[256,512]{1,0:T(8,128)(2,1)S(1)} %maximum_select_fusion.6), channel_id=1, source_target_pairs={{0,8},{8,0},{1,9},{9,1},{2,10},{10,2},{3,11},{11,3},{4,12},{12,4},... | collective-permute-start | bytes 786440 | tf_op jit(solution)/shard_map/ppermute | solution.py:21
  97.3 1528.5 %collective-permute-start.16 = (bf16[256,512]{1,0:T(8,128)(2,1)}, bf16[256,512]{1,0:T(8,128)(2,1)}, u32[]{:S(2)}, u32[]{:S(2)}) collective-permute-start(bf16[256,512]{1,0:T(8,128)(2,1)} %maximum_select_fusion.7), channel_id=1, source_target_pairs={{0,32},{32,0},{1,33},{33,1},{2,34},{34,2},{3,35},{35,3},{4,36},{36... | collective-permute-start | bytes 786440 | tf_op jit(solution)/shard_map/ppermute | solution.py:21
  125.0 1506.6 %collective-permute-start.5 = (bf16[512,512]{0,1:T(8,128)(2,1)S(1)}, bf16[512,512]{0,1:T(8,128)(2,1)S(1)}, u32[]{:S(2)}, u32[]{:S(2)}) collective-permute-start(bf16[512,512]{0,1:T(8,128)(2,1)S(1)} %maximum_select_fusion.3), channel_id=1, source_target_pairs={{0,2},{2,0},{1,3},{3,1},{4,6},{6,4},{5,7},{7,5},{8,10},{10,8},{9,1... | collective-permute-start | bytes 1572872 | tf_op jit(solution)/shard_map/ppermute | solution.py:21
  134.9 1494.9 %collective-permute-start.18 = (bf16[256,512]{0,1:T(8,128)(2,1)}, bf16[256,512]{0,1:T(8,128)(2,1)}, u32[]{:S(2)}, u32[]{:S(2)}) collective-permute-start(bf16[256,512]{0,1:T(8,128)(2,1)} %get-tuple-element.449), channel_id=1, source_target_pairs={{1,0},{2,1},{3,2},{4,3},{5,4},{6,5},{7,6},{8,7},{9,8},{10,9},{11,1... | collective-permute-start | bytes 786440 | tf_op jit(solution)/shard_map/ppermute | solution.py:27
  136.2 1493.6 %collective-permute-start.19 = (bf16[256,512]{0,1:T(8,128)(2,1)}, bf16[256,512]{0,1:T(8,128)(2,1)}, u32[]{:S(2)}, u32[]{:S(2)}) collective-permute-start(bf16[256,512]{0,1:T(8,128)(2,1)} %get-tuple-element.450), channel_id=1, source_target_pairs={{0,1},{1,2},{2,3},{3,4},{4,5},{5,6},{6,7},{7,8},{8,9},{9,10},{10,1... | collective-permute-start | bytes 786440 | tf_op jit(solution)/shard_map/ppermute | solution.py:27
  1623.8 21.8 %collective-permute-start.10 = (bf16[512,512]{1,0:T(8,128)(2,1)S(1)}, bf16[512,512]{1,0:T(8,128)(2,1)}, u32[]{:S(2)}, u32[]{:S(2)}) collective-permute-start(bf16[512,512]{1,0:T(8,128)(2,1)S(1)} %maximum_select_fusion.4), channel_id=1, source_target_pairs={{0,16},{16,0},{1,17},{17,1},{2,18},{18,2},{3,19},{19,3},{4,20},{20... | collective-permute-start | bytes 1572872 | tf_op jit(solution)/shard_map/ppermute | solution.py:21
  1627.8 36.8 %collective-permute-start.17 = (bf16[512,512]{1,0:T(8,128)(2,1)}, bf16[512,512]{1,0:T(8,128)(2,1)}, u32[]{:S(2)}, u32[]{:S(2)}) collective-permute-start(bf16[512,512]{1,0:T(8,128)(2,1)} %maximum_select_fusion.5), channel_id=1, source_target_pairs={{0,64},{64,0},{1,65},{65,1},{2,66},{66,2},{3,67},{67,3},{4,68},{68... | collective-permute-start | bytes 1572872 | tf_op jit(solution)/shard_map/ppermute | solution.py:21
  1642.4 57.1 %collective-permute-start.20 = (bf16[512,512]{0,1:T(8,128)(2,1)}, bf16[512,512]{0,1:T(8,128)(2,1)}, u32[]{:S(2)}, u32[]{:S(2)}) collective-permute-start(bf16[512,512]{0,1:T(8,128)(2,1)} %select_convert_fusion.2), channel_id=1, source_target_pairs={{0,2},{2,0},{1,3},{3,1},{4,6},{6,4},{5,7},{7,5},{8,10},{10,8},{9,1... | collective-permute-start | bytes 1572872 | tf_op jit(solution)/shard_map/ppermute | solution.py:21
  1656.5 47.3 %collective-permute-start.22 = (bf16[512,512]{1,0:T(8,128)(2,1)}, bf16[512,512]{1,0:T(8,128)(2,1)}, u32[]{:S(2)}, u32[]{:S(2)}) collective-permute-start(bf16[512,512]{1,0:T(8,128)(2,1)} %select_convert_fusion.1), channel_id=1, source_target_pairs={{0,16},{16,0},{1,17},{17,1},{2,18},{18,2},{3,19},{19,3},{4,20},{20... | collective-permute-start | bytes 1572872 | tf_op jit(solution)/shard_map/ppermute | solution.py:21
  1688.1 18.9 %collective-permute-start.27 = (bf16[512,512]{1,0:T(8,128)(2,1)}, bf16[512,512]{1,0:T(8,128)(2,1)}, u32[]{:S(2)}, u32[]{:S(2)}) collective-permute-start(bf16[512,512]{1,0:T(8,128)(2,1)} %select_convert_fusion), channel_id=1, source_target_pairs={{0,64},{64,0},{1,65},{65,1},{2,66},{66,2},{3,67},{67,3},{4,68},{68... | collective-permute-start | bytes 1572872 | tf_op jit(solution)/shard_map/ppermute | solution.py:21
  1701.1 9.3 collective-permute-start.21
  1705.1 9.2 collective-permute-start.23
  1708.4 8.3 collective-permute-start.28
  1714.5 6.9 collective-permute-start.24
  1716.8 12.4 collective-permute-start.29
  1721.4 11.6 collective-permute-start.25
  1729.3 7.9 collective-permute-start.30
  1733.1 6.7 collective-permute-start.26
  1743.1 9.5 collective-permute-start.32
  (121 other events, 815.8 us)
